TPU v7x, 256 devices: a whole 4x4x8 slice. The times are simulated.
256 devices in a mesh: wave: 8 (over z_hi, x), region: 32 (over z_lo, y, core).
Axes of the slice: x: 4, y: 4, z: 8 (z_hi: 2, z_lo: 4; z = z_hi * 4 + z_lo), core: 2. Of those that a mesh axis runs over, the one named last changes fastest.
Arguments:
- object_field: float32 [2, 16384, 1024], P(None, 'region'), may hold values from -5 to 5
- probes: float32 [8, 2, 256, 256], P('wave'), may hold values from -5 to 5
- patterns: bfloat16 [8, 512, 256, 256], P('wave', 'region'), may hold values from 0 to 2
- offsets: int32 [512, 2], P('region'), may hold values from 0 to 768, as said below
- counts: int32 [32], P('region'), may hold values from 1 to 16, as said below
Outputs:
- object_grad: float32 [2, 16384, 1024], P(None, 'region', 'wave')
- probe_grad: float32 [8, 2, 256, 256], P('wave')
Inputs may be any that keep to these rules, and one draw needn't show every extreme that they name: Offsets are whole cells: row offsets below 512, column offsets at most 768. `counts`: some tile uses all slots and some tile uses one.
All inputs are finite; a program needn't handle non-finite values.
Results may differ from a plain program's by a relative error of at most 0.0052.
Values sent between devices are 32-bit elements; how exact they have to be, the bound alone decides.
No kernel may reach another device: no remote copies, remote signals or barrier semaphores. Data moves between devices by JAX's collectives and lax.ppermute only.
A program may use at most 128 MiB of HBM per device.

v0:
```python
import math
import jax
import jax.numpy as jnp
from jax import lax
from jax.sharding import PartitionSpec as P


def from_behind(block, axis, distance):
    devices = range(lax.axis_size(axis))
    route = [(i - distance, i) for i in devices if i - distance in devices]
    return lax.ppermute(block, axis, route)


def make_tables(patch_side):
    index = jnp.arange(patch_side, dtype=jnp.int32)
    phase_int = index[:, None] * index[None, :] % patch_side
    phase = phase_int.astype(jnp.float32) * (2.0 * math.pi / patch_side)
    scale = 1.0 / math.sqrt(patch_side)
    return (
        (jnp.cos(phase) * scale).astype(jnp.bfloat16),
        (jnp.sin(phase) * scale).astype(jnp.bfloat16),
    )


def apply_left(table, field_part):
    return jnp.einsum("kn,bnm->bkm", table, field_part, preferred_element_type=jnp.float32)


def apply_right(field_part, table):
    return jnp.einsum("bkn,nm->bkm", field_part, table, preferred_element_type=jnp.float32)


def on_device(object_field, probes, patterns, offsets, counts):
    tile_rows = object_field.shape[1]
    width_cols = object_field.shape[2]
    patch_side = probes.shape[-1]
    slot_total = offsets.shape[0]
    top_rows = object_field[:, :patch_side, :]
    rim_rows = from_behind(top_rows, "region", -1)
    extended = jnp.concatenate([object_field, rim_rows], axis=1)
    zero_at = jnp.zeros((), jnp.int32)

    def extract(row_at, col_at):
        return lax.dynamic_slice(extended, (zero_at, row_at, col_at), (2, patch_side, patch_side))

    patches = jax.vmap(extract)(offsets[:, 0], offsets[:, 1])
    cos_table, sin_table = make_tables(patch_side)
    probe_re = probes[0, 0]
    probe_im = probes[0, 1]
    wave_re = (probe_re * patches[:, 0] - probe_im * patches[:, 1]).astype(jnp.bfloat16)
    wave_im = (probe_re * patches[:, 1] + probe_im * patches[:, 0]).astype(jnp.bfloat16)
    half_re = (apply_left(cos_table, wave_re) + apply_left(sin_table, wave_im)).astype(jnp.bfloat16)
    half_im = (apply_left(cos_table, wave_im) - apply_left(sin_table, wave_re)).astype(jnp.bfloat16)
    far_re = apply_right(half_re, cos_table) + apply_right(half_im, sin_table)
    far_im = apply_right(half_im, cos_table) - apply_right(half_re, sin_table)
    excess = far_re * far_re + far_im * far_im - patterns[0].astype(jnp.float32)
    back_re = (excess * far_re).astype(jnp.bfloat16)
    back_im = (excess * far_im).astype(jnp.bfloat16)
    inner_re = (apply_left(cos_table, back_re) - apply_left(sin_table, back_im)).astype(
        jnp.bfloat16
    )
    inner_im = (apply_left(cos_table, back_im) + apply_left(sin_table, back_re)).astype(
        jnp.bfloat16
    )
    chi_re = apply_right(inner_re, cos_table) - apply_right(inner_im, sin_table)
    chi_im = apply_right(inner_im, cos_table) + apply_right(inner_re, sin_table)
    in_use = (jnp.arange(slot_total, dtype=jnp.int32) < counts[0]).astype(jnp.float32)[
        :, None, None
    ]
    obj_terms = jnp.stack(
        [
            (probe_re * chi_re + probe_im * chi_im) * in_use,
            (probe_re * chi_im - probe_im * chi_re) * in_use,
        ],
        axis=1,
    )
    prb_re = jnp.sum((patches[:, 0] * chi_re + patches[:, 1] * chi_im) * in_use, axis=0)
    prb_im = jnp.sum((patches[:, 0] * chi_im - patches[:, 1] * chi_re) * in_use, axis=0)
    probe_total = lax.psum(jnp.stack([prb_re, prb_im]), "region")

    def accumulate(slot, grad_ext):
        row_at = offsets[slot, 0]
        col_at = offsets[slot, 1]
        current = lax.dynamic_slice(
            grad_ext, (zero_at, row_at, col_at), (2, patch_side, patch_side)
        )
        return lax.dynamic_update_slice(
            grad_ext, current + obj_terms[slot], (zero_at, row_at, col_at)
        )

    grad_ext = lax.fori_loop(
        0, slot_total, accumulate, jnp.zeros((2, tile_rows + patch_side, width_cols), jnp.float32)
    )
    arrived = from_behind(grad_ext[:, tile_rows:, :], "region", 1)
    tile_grad = grad_ext[:, :tile_rows, :] + jnp.pad(
        arrived, ((0, 0), (0, tile_rows - patch_side), (0, 0))
    )
    object_out = lax.psum_scatter(tile_grad, "wave", scatter_dimension=2, tiled=True)
    return (object_out, probe_total[None])


def solution(mesh):
    in_specs = (
        P(None, "region", None),
        P("wave", None, None, None),
        P("wave", "region", None, None),
        P("region", None),
        P("region"),
    )
    out_specs = (P(None, "region", "wave"), P("wave", None, None, None))
    return jax.shard_map(
        on_device, mesh=mesh, in_specs=in_specs, out_specs=out_specs, check_vma=False
    )
```

profile of v0, /device:TPU:1, one launch (start us, length us, event | category | flops | bytes accessed | tf_op | source)
XLA Modules:
  0.0 687.2 jit_solution(8466488751038629927)
XLA Ops:
  8.1 1.8 slice.34
  9.8 5.1 collective-permute-start
  15.8 22.5 %collective-permute-done = f32[2,256,1024]{2,1,0:T(8,128)} collective-permute-done((f32[2,256,1024]{2,1,0:T(8,128)S(1)}, f32[2,256,1024]{2,1,0:T(8,128)}, u32[]{:S(2)}, u32[]{:S(2)}) %collective-permute-start) | collective-permute-done | bytes 2097184 | tf_op jit(solution)/shard_map/ppermute | solution.py:11
  38.2 6.7 pad_maximum_fusion.1
  44.9 63.9 %while.15 = (s32[]{:T(128)}, f32[2,768,1024]{2,1,0:T(8,128)}, s32[16,3]{0,1:T(4,128)S(1)}, f32[16,2,256,256]{3,2,0,1:T(8,128)}, s32[]{:T(128)}) while((s32[]{:T(128)}, f32[2,768,1024]{2,1,0:T(8,128)}, s32[16,3]{0,1:T(4,128)S(1)}, f32[16,2,256,256]{3,2,0,1:T(8,128)}, s32[]{:T(128)}) %tuple.58), condition=%wide.while_cond, body=%wide.while_body.sunk | while | flops 2 | bytes 1050217 | solution.py:44
  45.5 3.3 bitcast_dynamic-update-slice_fusion.2
  49.5 3.3 bitcast_dynamic-update-slice_fusion.2
  53.5 3.4 bitcast_dynamic-update-slice_fusion.2
  57.5 3.4 bitcast_dynamic-update-slice_fusion.2
  61.5 3.4 bitcast_dynamic-update-slice_fusion.2
  65.5 3.4 bitcast_dynamic-update-slice_fusion.2
  69.5 3.4 bitcast_dynamic-update-slice_fusion.2
  73.5 3.4 bitcast_dynamic-update-slice_fusion.2
  77.5 3.3 bitcast_dynamic-update-slice_fusion.2
  81.5 3.4 bitcast_dynamic-update-slice_fusion.2
  85.5 3.4 bitcast_dynamic-update-slice_fusion.2
  89.5 3.3 bitcast_dynamic-update-slice_fusion.2
  93.4 3.3 bitcast_dynamic-update-slice_fusion.2
  97.4 3.3 bitcast_dynamic-update-slice_fusion.2
  101.4 3.4 bitcast_dynamic-update-slice_fusion.2
  105.4 3.4 bitcast_dynamic-update-slice_fusion.2
  108.8 4.7 fusion.3
  113.5 1.7 fusion.45
  115.1 1.7 fusion.48
  116.8 1.7 subtract_convert_fusion.1
  118.5 1.7 add_convert_fusion.1
  120.2 1.7 fusion.20
  121.9 1.7 fusion.16
  123.6 1.9 convolution_add_fusion.1
  125.5 2.9 multiply_convert_fusion
  128.4 1.7 fusion.42
  130.1 1.7 fusion.39
  131.7 1.7 subtract_convert_fusion
  133.5 1.7 add_convert_fusion
  135.1 1.7 fusion.10
  136.8 1.7 fusion.14
  138.5 1.7 convolution_add_fusion
  140.8 6.6 fusion.6
  147.4 4.1 pad_maximum_fusion
  151.5 3.5 broadcast_in_dim.4
  155.0 202.1 %while.14 = (s32[]{:T(128)}, f32[2,768,1024]{2,1,0:T(8,128)}, s32[16,2]{0,1:T(2,128)S(1)}, f32[16,2,256,256]{3,2,0,1:T(8,128)}, s32[]{:T(128)}, /*index=5*/s32[]{:T(128)}, s32[]{:T(128)}, s32[]{:T(128)}) while((s32[]{:T(128)}, f32[2,768,1024]{2,1,0:T(8,128)}, s32[16,2]{0,1:T(2,128)S(1)}, f32[16,2,256,256]{3,2,0,1:T(8,128)}, s32[]{:T(128)}, ...), condition=%wide.region_1.2_spmd, body=%wide.region_0.1_spmd.sunk | while | flops 131080 | bytes 2621629 | solution.py:91
  161.1 6.8 dynamic_update_slice.8
  173.8 6.8 dynamic_update_slice.8
  185.1 1.5 bitcast_add_fusion.2
  186.6 6.8 dynamic_update_slice.8
  199.4 6.2 dynamic_update_slice.8
  211.6 6.2 dynamic_update_slice.8
  223.8 6.8 dynamic_update_slice.8
  236.6 6.7 dynamic_update_slice.8
  249.3 6.8 dynamic_update_slice.8
  262.1 6.8 dynamic_update_slice.8
  274.9 6.5 dynamic_update_slice.8
  287.4 6.1 dynamic_update_slice.8
  299.5 6.8 dynamic_update_slice.8
  312.3 6.5 dynamic_update_slice.8
  324.8 6.8 dynamic_update_slice.8
  337.6 6.7 dynamic_update_slice.8
  350.3 6.8 dynamic_update_slice.8
  357.1 3.2 slice.41
  360.4 1.9 collective-permute-start.1
  363.2 22.5 %collective-permute-done.1 = f32[2,256,1024]{2,1,0:T(8,128)S(1)} collective-permute-done((f32[2,256,1024]{2,1,0:T(8,128)}, f32[2,256,1024]{2,1,0:T(8,128)S(1)}, u32[]{:S(2)}, u32[]{:S(2)}) %collective-permute-start.1) | collective-permute-done | bytes 2097184 | tf_op jit(solution)/shard_map/ppermute | solution.py:11
  385.7 5.0 pad_add_fusion
  390.8 287.1 %all-reduce.3.cloned.1.call-done = f32[1,2,256,256]{3,2,1,0:T(8,128)} async-done(((f32[1,2,256,256]{3,2,1,0:T(8,128)}), f32[1,2,256,256]{3,2,1,0:T(8,128)}) %all-reduce.3.cloned.1.call-update) | async-done | bytes 524304 | tf_op jit(solution)/shard_map/psum | solution.py:79
  677.9 1.9 copy.64
  (94 shorter events, 44.3 us)
Async XLA Ops:
  8.0 7.6 %copy-start.6 = (s32[16,2]{0,1:T(2,128)S(1)}, s32[16,2]{0,1:T(2,128)}, u32[]{:S(2)}) copy-start(s32[16,2]{0,1:T(2,128)} %param.10) | copy-start | bytes 388
  8.0 7.7 %copy-start.3 = (f32[1,2,256,256]{3,2,1,0:T(8,128)S(1)}, f32[1,2,256,256]{3,2,1,0:T(8,128)}, u32[]{:S(2)}) copy-start(f32[1,2,256,256]{3,2,1,0:T(8,128)} %param.8) | copy-start | bytes 1572868
  8.0 669.9 %all-reduce.3.cloned.1.call-start = ((), (), s32[]{:S(2)}) async-start(), calls=%async_computation.2 | async-start | bytes 1048576 | tf_op jit(solution)/shard_map/psum | solution.py:79
  9.8 28.4 %collective-permute-start = (f32[2,256,1024]{2,1,0:T(8,128)S(1)}, f32[2,256,1024]{2,1,0:T(8,128)}, u32[]{:S(2)}, u32[]{:S(2)}) collective-permute-start(f32[2,256,1024]{2,1,0:T(8,128)S(1)} %slice.34), channel_id=1, source_target_pairs={{1,0},{2,1},{3,2},{4,3},{5,4},{6,5},{7,6},{8,7},{9,8},{10,9},{11,1... | collective-permute-start | bytes 6291464 | tf_op jit(solution)/shard_map/ppermute | solution.py:11
  15.7 93.0 %copy-start.1 = (f32[256,256]{1,0:T(8,128)}, f32[256,256]{1,0:T(8,128)S(1)}, u32[]{:S(2)}) copy-start(f32[256,256]{1,0:T(8,128)S(1)} %get-tuple-element.124) | copy-start | bytes 786436
  15.7 93.0 %copy-start.2 = (f32[256,256]{1,0:T(8,128)}, f32[256,256]{1,0:T(8,128)S(1)}, u32[]{:S(2)}) copy-start(f32[256,256]{1,0:T(8,128)S(1)} %get-tuple-element.125) | copy-start | bytes 786436
  123.6 1.9 copy-start
  136.8 3.4 slice-start
  138.5 2.3 slice-start.1
  357.1 5.2 copy-start.4
  357.1 5.2 copy-start.5
  360.4 25.4 %collective-permute-start.1 = (f32[2,256,1024]{2,1,0:T(8,128)}, f32[2,256,1024]{2,1,0:T(8,128)S(1)}, u32[]{:S(2)}, u32[]{:S(2)}) collective-permute-start(f32[2,256,1024]{2,1,0:T(8,128)} %slice.41), channel_id=1, source_target_pairs={{0,1},{1,2},{2,3},{3,4},{4,5},{5,6},{6,7},{7,8},{8,9},{9,10},{10,1... | collective-permute-start | bytes 6291464 | tf_op jit(solution)/shard_map/ppermute | solution.py:11
  363.2 314.7 %reduce-scatter.2.cloned.1.call-start = ((), (), s32[]{:S(2)}) async-start(), calls=%async_computation.1 | async-start | bytes 4718592 | tf_op jit(solution)/shard_map/reduce_scatter | solution.py:98
Sparse Core Ops, SparseCore 0:
  363.3 314.5 all-reduce.2
Sparse Core Ops, SparseCore 1:
  390.8 125.0 reduce-scatter.1
where the time goes:
time: 692 us; the launch traced here: 687 us
  waiting for transfers between devices  332 us (48%)
  local copies, waits for them, and re-layouts  190 us (27%)
  loops' own time  62.2 us (9%)
  other arithmetic  45.8 us (7%)
  matrix products  33.2 us (5%)
  between operations  16.4 us (2%)
  starting transfers between devices  7.1 us (1%)
    psum x1, waiting for transfers between devices, on_device(): probe_total = lax.psum(jnp.stack([prb_re, prb_im]), 'region')  287 us
    dynamic_update_slice x16, local copies, waits for them, and re-layouts, accumulate(): lax.dynamic_update_slice(grad_ext, current + obj_terms[slot], (zero_at, r...  106 us
    gather x48, local copies, waits for them, and re-layouts  63.9 us
    another operation x1, loops' own time, on_device(): lax.fori_loop(0, slot_total, accumulate, jnp.zeros((2, tile_rows + patch_...  62.2 us
    ppermute x2, waiting for transfers between devices, from_behind(): return lax.ppermute(block, axis, route)  45 us
    add x16, other arithmetic, accumulate(): current + obj_terms[slot]  24.5 us
    dot_general x8, matrix products, apply_right(): jnp.einsum('bkn,nm->bkm', field_part, table, preferred_element_type=jnp.f...  19.7 us
  transfers between devices with their start and end apart: 4, of which 3 were waited for; matrix products, arithmetic and copies ran while one was open for 1% of the time, Pallas kernels for 0%

commit v1 on v0

--- a/solution.py
+++ b/solution.py
@@ -76,7 +76,7 @@
     )
     prb_re = jnp.sum((patches[:, 0] * chi_re + patches[:, 1] * chi_im) * in_use, axis=0)
     prb_im = jnp.sum((patches[:, 0] * chi_im - patches[:, 1] * chi_re) * in_use, axis=0)
-    probe_total = lax.psum(jnp.stack([prb_re, prb_im]), "region")
+    probe_total = jnp.sum(lax.all_gather(jnp.stack([prb_re, prb_im]), "region"), axis=0)
 
     def accumulate(slot, grad_ext):
         row_at = offsets[slot, 0]

time: 692 us -> 541 us (0.78)
  waiting for transfers between devices: 332 us -> 165 us
  other arithmetic: 45.8 us -> 57.5 us
    psum x1 -> x0, waiting for transfers between devices: 287 us -> none  [on_device(): probe_total = lax.psum(jnp.stack([prb_re, prb_im]), 'region')]
    reduce_scatter x1, waiting for transfers between devices: 0.01 us -> 120 us  [on_device(): lax.psum_scatter(tile_grad, 'wave', scatter_dimension=2, tiled=True)]
    reduce_sum x0 -> x1, other arithmetic: none -> 7.69 us  [on_device(): jnp.sum(lax.all_gather(jnp.stack([prb_re, prb_im]), 'region'), axis=0)]
  transfers between devices with their start and end apart: 4 -> 4, of which waited for: 3 -> 3; matrix products, arithmetic and copies ran while one was open for 1% -> 31% of each run, Pallas kernels for 0% -> 0%
where the time goes in v1:
time: 541 us; the launch traced here: 535 us
  local copies, waits for them, and re-layouts  191 us (35%)
  waiting for transfers between devices  165 us (30%)
  loops' own time  63.8 us (12%)
  other arithmetic  57.5 us (11%)
  matrix products  34 us (6%)
  between operations  16.4 us (3%)
  starting transfers between devices  7.11 us (1%)
    reduce_scatter x1, waiting for transfers between devices, on_device(): lax.psum_scatter(tile_grad, 'wave', scatter_dimension=2, tiled=True)  120 us
    dynamic_update_slice x16, local copies, waits for them, and re-layouts, accumulate(): lax.dynamic_update_slice(grad_ext, current + obj_terms[slot], (zero_at, r...  106 us
    gather x48, local copies, waits for them, and re-layouts  66.6 us
    another operation x1, loops' own time, on_device(): lax.fori_loop(0, slot_total, accumulate, jnp.zeros((2, tile_rows + patch_...  63.8 us
    ppermute x2, waiting for transfers between devices, from_behind(): return lax.ppermute(block, axis, route)  45.5 us
    add x16, other arithmetic, accumulate(): current + obj_terms[slot]  25 us
    dot_general x8, matrix products, apply_right(): jnp.einsum('bkn,nm->bkm', field_part, table, preferred_element_type=jnp.f...  20.5 us
    dot_general x8, matrix products, apply_left(): jnp.einsum('kn,bnm->bkm', table, field_part, preferred_element_type=jnp.f...  13.5 us
  transfers between devices with their start and end apart: 4, of which 3 were waited for; matrix products, arithmetic and copies ran while one was open for 31% of the time, Pallas kernels for 0%

profile of v1, /device:TPU:1, one launch (start us, length us, event | category | flops | bytes accessed | tf_op | source)
XLA Modules:
  0.0 534.8 jit_solution(3981517262395758004)
XLA Ops:
  8.1 1.8 slice.34
  9.8 5.1 collective-permute-start
  15.7 22.5 %collective-permute-done = f32[2,256,1024]{2,1,0:T(8,128)} collective-permute-done((f32[2,256,1024]{2,1,0:T(8,128)S(1)}, f32[2,256,1024]{2,1,0:T(8,128)}, u32[]{:S(2)}, u32[]{:S(2)}) %collective-permute-start) | collective-permute-done | bytes 2097184 | tf_op jit(solution)/shard_map/ppermute | solution.py:11
  38.2 6.6 %pad_maximum_fusion.1 = f32[2,768,1024]{2,1,0:T(8,128)} fusion(f32[2,256,1024]{2,1,0:T(8,128)} %collective-permute-done, f32[2,512,1024]{2,1,0:T(8,128)} %param.7), kind=kLoop, calls=%fused_computation.6 | loop fusion | flops 1572864 | bytes 12582912 | tf_op jit(solution)/shard_map/concatenate | solution.py:40
  44.9 66.6 %while.15 = (s32[]{:T(128)}, f32[2,768,1024]{2,1,0:T(8,128)}, s32[16,3]{0,1:T(4,128)S(1)}, f32[16,2,256,256]{3,2,0,1:T(8,128)}, s32[]{:T(128)}) while((s32[]{:T(128)}, f32[2,768,1024]{2,1,0:T(8,128)}, s32[16,3]{0,1:T(4,128)S(1)}, f32[16,2,256,256]{3,2,0,1:T(8,128)}, s32[]{:T(128)}) %tuple.59), condition=%wide.while_cond, body=%wide.while_body.sunk | while | flops 2 | bytes 1050217 | solution.py:44
  45.6 3.5 bitcast_dynamic-update-slice_fusion.2
  49.7 3.5 bitcast_dynamic-update-slice_fusion.2
  53.9 3.5 bitcast_dynamic-update-slice_fusion.2
  58.1 3.5 bitcast_dynamic-update-slice_fusion.2
  62.2 3.5 bitcast_dynamic-update-slice_fusion.2
  66.4 3.5 bitcast_dynamic-update-slice_fusion.2
  70.6 3.5 bitcast_dynamic-update-slice_fusion.2
  74.7 3.5 bitcast_dynamic-update-slice_fusion.2
  78.9 3.5 bitcast_dynamic-update-slice_fusion.2
  83.0 3.5 bitcast_dynamic-update-slice_fusion.2
  87.2 3.5 bitcast_dynamic-update-slice_fusion.2
  91.3 3.5 bitcast_dynamic-update-slice_fusion.2
  95.5 3.5 bitcast_dynamic-update-slice_fusion.2
  99.6 3.5 bitcast_dynamic-update-slice_fusion.2
  103.8 3.5 bitcast_dynamic-update-slice_fusion.2
  108.0 3.5 bitcast_dynamic-update-slice_fusion.2
  111.5 4.7 fusion.3
  116.2 1.7 fusion.45
  117.8 1.7 fusion.48
  119.5 1.7 subtract_convert_fusion.1
  121.2 1.7 add_convert_fusion.1
  122.9 1.7 fusion.20
  124.6 1.7 fusion.16
  126.3 1.9 convolution_add_fusion.1
  128.2 2.9 multiply_convert_fusion
  131.1 1.7 fusion.42
  132.8 1.7 fusion.39
  134.4 1.7 subtract_convert_fusion
  136.2 1.7 add_convert_fusion
  137.8 1.7 fusion.10
  139.5 1.7 fusion.14
  141.2 1.7 convolution_add_fusion
  143.5 7.4 %fusion.6 = (f32[256,256]{1,0:T(8,128)S(1)}, f32[256,256]{1,0:T(8,128)S(1)}, f32[16,1,256,256]{3,2,0,1:T(8,128)}, f32[16,1,256,256]{3,2,0,1:T(8,128)}) fusion(f32[16,256,256]{2,1,0:T(8,128)S(1)} %convolution_add_fusion, f32[16,2,256,256]{3,2,0,1:T(8,128)S(1)} %bitcast.138, f32[16]{0:T(128)S(1)} %compare_convert_fusion, ...), kind=kOutput, calls=%fused_computation.18 | convolution fusion | flops 557711360 | bytes 28311616 | tf_op jit(solution)/shard_map/bkn,nm->bkm/dot_general | solution.py:30
  151.8 7.6 %pad_maximum_fusion = f32[16,2,256,256]{3,2,0,1:T(8,128)} fusion(f32[16,1,256,256]{3,2,0,1:T(8,128)} %get-tuple-element.126, f32[16,1,256,256]{3,2,0,1:T(8,128)} %get-tuple-element.127), kind=kLoop, calls=%fused_computation.5 | loop fusion | flops 2097152 | bytes 16777216 | tf_op jit(solution)/shard_map/stack | solution.py:70
  159.4 3.5 broadcast_in_dim.4
  162.9 205.5 %while.14 = (s32[]{:T(128)}, f32[2,768,1024]{2,1,0:T(8,128)}, s32[16,2]{0,1:T(2,128)S(1)}, f32[16,2,256,256]{3,2,0,1:T(8,128)}, s32[]{:T(128)}, /*index=5*/s32[]{:T(128)}, s32[]{:T(128)}, s32[]{:T(128)}) while((s32[]{:T(128)}, f32[2,768,1024]{2,1,0:T(8,128)}, s32[16,2]{0,1:T(2,128)S(1)}, f32[16,2,256,256]{3,2,0,1:T(8,128)}, s32[]{:T(128)}, ...), condition=%wide.region_1.2_spmd, body=%wide.region_0.1_spmd.sunk | while | flops 131080 | bytes 2621629 | solution.py:91
  167.5 1.8 bitcast_add_fusion.2
  169.3 6.8 %dynamic_update_slice.8 = f32[2,768,1024]{2,1,0:T(8,128)} dynamic-update-slice(f32[2,768,1024]{2,1,0:T(8,128)} %get-tuple-element.214, f32[2,256,256]{2,1,0:T(8,128)S(1)} %bitcast_add_fusion.2, s32[]{:T(128)} %constant.56.clone.1..sunk, s32[]{:T(128)S(6)} %select_n.104, s32[]{:T(128)S(6)} %select_n.105) | dynamic-update-slice | bytes 1048580 | tf_op jit(solution)/shard_map/while/body/eval_jaxpr/dynamic_update_slice | solution.py:87
  182.2 6.8 %dynamic_update_slice.8 = f32[2,768,1024]{2,1,0:T(8,128)} dynamic-update-slice(f32[2,768,1024]{2,1,0:T(8,128)} %get-tuple-element.214, f32[2,256,256]{2,1,0:T(8,128)S(1)} %bitcast_add_fusion.2, s32[]{:T(128)} %constant.56.clone.1..sunk, s32[]{:T(128)S(6)} %select_n.104, s32[]{:T(128)S(6)} %select_n.105) | dynamic-update-slice | bytes 1048580 | tf_op jit(solution)/shard_map/while/body/eval_jaxpr/dynamic_update_slice | solution.py:87
  195.3 6.8 %dynamic_update_slice.8 = f32[2,768,1024]{2,1,0:T(8,128)} dynamic-update-slice(f32[2,768,1024]{2,1,0:T(8,128)} %get-tuple-element.214, f32[2,256,256]{2,1,0:T(8,128)S(1)} %bitcast_add_fusion.2, s32[]{:T(128)} %constant.56.clone.1..sunk, s32[]{:T(128)S(6)} %select_n.104, s32[]{:T(128)S(6)} %select_n.105) | dynamic-update-slice | bytes 1048580 | tf_op jit(solution)/shard_map/while/body/eval_jaxpr/dynamic_update_slice | solution.py:87
  208.3 6.2 %dynamic_update_slice.8 = f32[2,768,1024]{2,1,0:T(8,128)} dynamic-update-slice(f32[2,768,1024]{2,1,0:T(8,128)} %get-tuple-element.214, f32[2,256,256]{2,1,0:T(8,128)S(1)} %bitcast_add_fusion.2, s32[]{:T(128)} %constant.56.clone.1..sunk, s32[]{:T(128)S(6)} %select_n.104, s32[]{:T(128)S(6)} %select_n.105) | dynamic-update-slice | bytes 1048580 | tf_op jit(solution)/shard_map/while/body/eval_jaxpr/dynamic_update_slice | solution.py:87
  220.7 6.2 %dynamic_update_slice.8 = f32[2,768,1024]{2,1,0:T(8,128)} dynamic-update-slice(f32[2,768,1024]{2,1,0:T(8,128)} %get-tuple-element.214, f32[2,256,256]{2,1,0:T(8,128)S(1)} %bitcast_add_fusion.2, s32[]{:T(128)} %constant.56.clone.1..sunk, s32[]{:T(128)S(6)} %select_n.104, s32[]{:T(128)S(6)} %select_n.105) | dynamic-update-slice | bytes 1048580 | tf_op jit(solution)/shard_map/while/body/eval_jaxpr/dynamic_update_slice | solution.py:87
  233.2 6.8 %dynamic_update_slice.8 = f32[2,768,1024]{2,1,0:T(8,128)} dynamic-update-slice(f32[2,768,1024]{2,1,0:T(8,128)} %get-tuple-element.214, f32[2,256,256]{2,1,0:T(8,128)S(1)} %bitcast_add_fusion.2, s32[]{:T(128)} %constant.56.clone.1..sunk, s32[]{:T(128)S(6)} %select_n.104, s32[]{:T(128)S(6)} %select_n.105) | dynamic-update-slice | bytes 1048580 | tf_op jit(solution)/shard_map/while/body/eval_jaxpr/dynamic_update_slice | solution.py:87
  246.2 6.7 %dynamic_update_slice.8 = f32[2,768,1024]{2,1,0:T(8,128)} dynamic-update-slice(f32[2,768,1024]{2,1,0:T(8,128)} %get-tuple-element.214, f32[2,256,256]{2,1,0:T(8,128)S(1)} %bitcast_add_fusion.2, s32[]{:T(128)} %constant.56.clone.1..sunk, s32[]{:T(128)S(6)} %select_n.104, s32[]{:T(128)S(6)} %select_n.105) | dynamic-update-slice | bytes 1048580 | tf_op jit(solution)/shard_map/while/body/eval_jaxpr/dynamic_update_slice | solution.py:87
  259.1 6.8 %dynamic_update_slice.8 = f32[2,768,1024]{2,1,0:T(8,128)} dynamic-update-slice(f32[2,768,1024]{2,1,0:T(8,128)} %get-tuple-element.214, f32[2,256,256]{2,1,0:T(8,128)S(1)} %bitcast_add_fusion.2, s32[]{:T(128)} %constant.56.clone.1..sunk, s32[]{:T(128)S(6)} %select_n.104, s32[]{:T(128)S(6)} %select_n.105) | dynamic-update-slice | bytes 1048580 | tf_op jit(solution)/shard_map/while/body/eval_jaxpr/dynamic_update_slice | solution.py:87
  272.0 6.8 %dynamic_update_slice.8 = f32[2,768,1024]{2,1,0:T(8,128)} dynamic-update-slice(f32[2,768,1024]{2,1,0:T(8,128)} %get-tuple-element.214, f32[2,256,256]{2,1,0:T(8,128)S(1)} %bitcast_add_fusion.2, s32[]{:T(128)} %constant.56.clone.1..sunk, s32[]{:T(128)S(6)} %select_n.104, s32[]{:T(128)S(6)} %select_n.105) | dynamic-update-slice | bytes 1048580 | tf_op jit(solution)/shard_map/while/body/eval_jaxpr/dynamic_update_slice | solution.py:87
  285.0 6.5 %dynamic_update_slice.8 = f32[2,768,1024]{2,1,0:T(8,128)} dynamic-update-slice(f32[2,768,1024]{2,1,0:T(8,128)} %get-tuple-element.214, f32[2,256,256]{2,1,0:T(8,128)S(1)} %bitcast_add_fusion.2, s32[]{:T(128)} %constant.56.clone.1..sunk, s32[]{:T(128)S(6)} %select_n.104, s32[]{:T(128)S(6)} %select_n.105) | dynamic-update-slice | bytes 1048580 | tf_op jit(solution)/shard_map/while/body/eval_jaxpr/dynamic_update_slice | solution.py:87
  297.7 6.1 %dynamic_update_slice.8 = f32[2,768,1024]{2,1,0:T(8,128)} dynamic-update-slice(f32[2,768,1024]{2,1,0:T(8,128)} %get-tuple-element.214, f32[2,256,256]{2,1,0:T(8,128)S(1)} %bitcast_add_fusion.2, s32[]{:T(128)} %constant.56.clone.1..sunk, s32[]{:T(128)S(6)} %select_n.104, s32[]{:T(128)S(6)} %select_n.105) | dynamic-update-slice | bytes 1048580 | tf_op jit(solution)/shard_map/while/body/eval_jaxpr/dynamic_update_slice | solution.py:87
  310.0 6.8 %dynamic_update_slice.8 = f32[2,768,1024]{2,1,0:T(8,128)} dynamic-update-slice(f32[2,768,1024]{2,1,0:T(8,128)} %get-tuple-element.214, f32[2,256,256]{2,1,0:T(8,128)S(1)} %bitcast_add_fusion.2, s32[]{:T(128)} %constant.56.clone.1..sunk, s32[]{:T(128)S(6)} %select_n.104, s32[]{:T(128)S(6)} %select_n.105) | dynamic-update-slice | bytes 1048580 | tf_op jit(solution)/shard_map/while/body/eval_jaxpr/dynamic_update_slice | solution.py:87
  323.0 6.5 %dynamic_update_slice.8 = f32[2,768,1024]{2,1,0:T(8,128)} dynamic-update-slice(f32[2,768,1024]{2,1,0:T(8,128)} %get-tuple-element.214, f32[2,256,256]{2,1,0:T(8,128)S(1)} %bitcast_add_fusion.2, s32[]{:T(128)} %constant.56.clone.1..sunk, s32[]{:T(128)S(6)} %select_n.104, s32[]{:T(128)S(6)} %select_n.105) | dynamic-update-slice | bytes 1048580 | tf_op jit(solution)/shard_map/while/body/eval_jaxpr/dynamic_update_slice | solution.py:87
  335.7 6.8 %dynamic_update_slice.8 = f32[2,768,1024]{2,1,0:T(8,128)} dynamic-update-slice(f32[2,768,1024]{2,1,0:T(8,128)} %get-tuple-element.214, f32[2,256,256]{2,1,0:T(8,128)S(1)} %bitcast_add_fusion.2, s32[]{:T(128)} %constant.56.clone.1..sunk, s32[]{:T(128)S(6)} %select_n.104, s32[]{:T(128)S(6)} %select_n.105) | dynamic-update-slice | bytes 1048580 | tf_op jit(solution)/shard_map/while/body/eval_jaxpr/dynamic_update_slice | solution.py:87
  348.6 6.7 %dynamic_update_slice.8 = f32[2,768,1024]{2,1,0:T(8,128)} dynamic-update-slice(f32[2,768,1024]{2,1,0:T(8,128)} %get-tuple-element.214, f32[2,256,256]{2,1,0:T(8,128)S(1)} %bitcast_add_fusion.2, s32[]{:T(128)} %constant.56.clone.1..sunk, s32[]{:T(128)S(6)} %select_n.104, s32[]{:T(128)S(6)} %select_n.105) | dynamic-update-slice | bytes 1048580 | tf_op jit(solution)/shard_map/while/body/eval_jaxpr/dynamic_update_slice | solution.py:87
  361.5 6.8 %dynamic_update_slice.8 = f32[2,768,1024]{2,1,0:T(8,128)} dynamic-update-slice(f32[2,768,1024]{2,1,0:T(8,128)} %get-tuple-element.214, f32[2,256,256]{2,1,0:T(8,128)S(1)} %bitcast_add_fusion.2, s32[]{:T(128)} %constant.56.clone.1..sunk, s32[]{:T(128)S(6)} %select_n.104, s32[]{:T(128)S(6)} %select_n.105) | dynamic-update-slice | bytes 1048580 | tf_op jit(solution)/shard_map/while/body/eval_jaxpr/dynamic_update_slice | solution.py:87
  368.3 1.7 slice.41
  370.0 1.9 collective-permute-start.1
  372.0 23.0 %collective-permute-done.1 = f32[2,256,1024]{2,1,0:T(8,128)S(1)} collective-permute-done((f32[2,256,1024]{2,1,0:T(8,128)S(1)}, f32[2,256,1024]{2,1,0:T(8,128)S(1)}, u32[]{:S(2)}, u32[]{:S(2)}) %collective-permute-start.1) | collective-permute-done | bytes 2097184 | tf_op jit(solution)/shard_map/ppermute | solution.py:11
  394.9 5.1 pad_add_fusion
  400.1 7.7 %reduce_sum.29 = f32[2,256,256]{2,1,0:T(8,128)} reduce(f32[32,2,256,256]{3,2,1,0:T(8,128)} %bitcast.136, f32[]{:T(128)} %constant.57.clone.1), dimensions={0}, to_apply=%region_5.6 | reduce | flops 4063232 | bytes 17301508 | tf_op jit(solution)/shard_map/reduce_sum | solution.py:79
  407.8 119.6 %reduce-scatter.2.cloned.1.call-done = f32[2,512,128]{2,1,0:T(8,128)} async-done(((f32[2,512,1024]{2,1,0:T(8,128)}), f32[2,512,128]{2,1,0:T(8,128)}) %reduce-scatter.2.cloned.1.call-update) | async-done | bytes 524304 | tf_op jit(solution)/shard_map/reduce_scatter | solution.py:98
  (86 shorter events, 46.2 us)
Async XLA Ops:
  8.0 7.6 %copy-start.2 = (s32[16,2]{0,1:T(2,128)S(1)}, s32[16,2]{0,1:T(2,128)}, u32[]{:S(2)}) copy-start(s32[16,2]{0,1:T(2,128)} %param.10) | copy-start | bytes 388
  8.0 7.7 %copy-start.1 = (f32[1,2,256,256]{3,2,1,0:T(8,128)S(1)}, f32[1,2,256,256]{3,2,1,0:T(8,128)}, u32[]{:S(2)}) copy-start(f32[1,2,256,256]{3,2,1,0:T(8,128)} %param.8) | copy-start | bytes 1572868
  8.0 392.0 %all-gather.3.cloned.1.call-start = ((), (), s32[]{:S(2)}) async-start(), calls=%async_computation.2 | async-start | bytes 17301504 | tf_op jit(solution)/shard_map/all_gather | solution.py:79
  9.8 28.4 %collective-permute-start = (f32[2,256,1024]{2,1,0:T(8,128)S(1)}, f32[2,256,1024]{2,1,0:T(8,128)}, u32[]{:S(2)}, u32[]{:S(2)}) collective-permute-start(f32[2,256,1024]{2,1,0:T(8,128)S(1)} %slice.34), channel_id=1, source_target_pairs={{1,0},{2,1},{3,2},{4,3},{5,4},{6,5},{7,6},{8,7},{9,8},{10,9},{11,1... | collective-permute-start | bytes 6291464 | tf_op jit(solution)/shard_map/ppermute | solution.py:11
  126.3 1.9 copy-start
  139.5 3.4 slice-start
  141.2 2.3 slice-start.1
  151.8 375.6 %reduce-scatter.2.cloned.1.call-start = ((), (), s32[]{:S(2)}) async-start(), calls=%async_computation.1 | async-start | bytes 4718592 | tf_op jit(solution)/shard_map/reduce_scatter | solution.py:98
  370.0 24.9 %collective-permute-start.1 = (f32[2,256,1024]{2,1,0:T(8,128)S(1)}, f32[2,256,1024]{2,1,0:T(8,128)S(1)}, u32[]{:S(2)}, u32[]{:S(2)}) collective-permute-start(f32[2,256,1024]{2,1,0:T(8,128)S(1)} %slice.41), channel_id=1, source_target_pairs={{0,1},{1,2},{2,3},{3,4},{4,5},{5,6},{6,7},{7,8},{8,9},{9,10},{10,1... | collective-permute-start | bytes 6291464 | tf_op jit(solution)/shard_map/ppermute | solution.py:11
Sparse Core Ops, SparseCore 0:
  151.9 104.3 all-gather.2
Sparse Core Ops, SparseCore 1:
  400.1 127.2 reduce-scatter.1
